TPU v7x, 256 devices: a whole 4x4x8 slice. The times are simulated.
256 devices in a mesh: blk: 32 (over z, y), group: 8 (over x, core).
Axes of the slice: x: 4, y: 4, z: 8, core: 2. Of those that a mesh axis runs over, the one named last changes fastest.
Arguments:
- queries: bfloat16 [32, 2048, 2560], P('blk', 'group'), may hold values from -16 to 16
- new_kv: bfloat16 [32, 2048, 512], P('blk', 'group'), may hold values from -16 to 16
- kv_pool: bfloat16 [1024, 128, 512], P('blk'), may hold values from -16 to 16
- window_table: int32 [32, 16], replicated, may hold values from 0 to 1023, as said below
- append_table: int32 [32, 16], replicated, may hold values from 0 to 1023, as said below
- cache_lengths: int32 [32], replicated, may hold values from 0 to 16384, as said below
Outputs:
- attn_out: bfloat16 [32, 2048, 2560], P('blk', 'group')
- new_pool: bfloat16 [1024, 128, 512], P('blk')
Inputs may be any that keep to these rules, and one draw needn't show every extreme that they name: `window_table`: pool page p lies on blk index p // 32. The two tables together name every pool page exactly once. For each k, each blk index holds window page k of exactly one request; at most 1 window pages of one request lie on one blk index, and some request has that many there. `append_table`: for each k, each blk index receives appended page k of exactly one request; at most one appended page of one request goes to one blk index, and some request sends one there. `cache_lengths`: A multiple of 128; some request has no cached token and some has 16384.
All inputs are finite; a program needn't handle non-finite values.
Results may differ from a plain program's by a relative error of at most 0.0043.
Values may be sent and summed in bfloat16 or wider, within the bound.
No kernel may reach another device: no remote copies, remote signals or barrier semaphores. Data moves between devices by JAX's collectives and lax.ppermute only.
A program may use at most 128 MiB of HBM per device.

v0:
```python
import jax
import jax.numpy as jnp
from jax import lax
from jax.sharding import PartitionSpec as P


def earlier_same(owners):
    slot_count = owners.shape[1]
    same_owner = owners[:, :, None] == owners[:, None, :]
    before = jnp.arange(slot_count)[None, :] < jnp.arange(slot_count)[:, None]
    return jnp.sum(same_owner & before[None, :, :], axis=2)


def pick_rows(wanted, values):
    return jnp.sum(jnp.where(wanted, values[:, None, :], 0), axis=2)


def attend(qblock, keys_use, index_use, live_use, block_start, head_count, head_size, window_len):
    block_len = qblock.shape[0]
    query_rows = qblock.reshape(block_len, head_count, head_size)
    scores = jnp.einsum(
        "thd,kd->thk", query_rows, keys_use[:, :head_size], preferred_element_type=jnp.float32
    ) * head_size ** (-0.5)
    positions = block_start + jnp.arange(block_len)
    allowed = (
        (index_use[None, :] > positions[:, None])
        & (index_use[None, :] <= positions[:, None] + window_len)
        & live_use[None, :]
    )
    scores = jnp.where(allowed[:, None, :], scores, -jnp.inf)
    row_max = jnp.max(scores, axis=2, keepdims=True)
    raw_weights = jnp.exp(scores - row_max)
    row_total = jnp.sum(raw_weights, axis=2, keepdims=True)
    weights = raw_weights.astype(jnp.bfloat16)
    weighted = jnp.einsum(
        "thk,kd->thd", weights, keys_use[:, head_size:], preferred_element_type=jnp.float32
    )
    return (weighted / row_total).astype(jnp.bfloat16).reshape(block_len, head_count * head_size)


def shards(queries, new_kv, kv_pool, window_table, append_table, cache_lengths):
    blocks = lax.axis_size("blk")
    my_block = lax.axis_index("blk")
    piece_index = lax.axis_index("group")
    tok_rows = queries.shape[1]
    per_owner = kv_pool.shape[0]
    page_rows = kv_pool.shape[1]
    key_width = kv_pool.shape[2]
    head_size = key_width // 2
    head_count = queries.shape[2] // head_size
    win_pages = window_table.shape[1]
    new_pages = append_table.shape[1]
    win_rows = win_pages * page_rows
    cap_win = (win_pages + blocks - 1) // blocks
    cap_new = (new_pages + blocks - 1) // blocks
    fresh_keys = lax.all_gather(new_kv, "group", axis=1, tiled=True)[0]
    append_rows = fresh_keys.shape[0]
    win_owner = window_table // per_owner
    win_rank = earlier_same(win_owner)
    win_wanted = (win_owner == my_block)[:, None, :] & (
        win_rank[:, None, :] == jnp.arange(cap_win)[None, :, None]
    )
    send_ids = pick_rows(win_wanted, window_table % per_owner)
    send_live = jnp.any(win_wanted, axis=2)
    own_owner = lax.dynamic_index_in_dim(win_owner, my_block, 0, keepdims=False)
    own_rank = lax.dynamic_index_in_dim(win_rank, my_block, 0, keepdims=False)
    arrival = own_owner * cap_win + own_rank
    outgoing = jnp.where(send_live[:, :, None, None], kv_pool[send_ids], 0)
    received = lax.all_to_all(
        outgoing.reshape(blocks * cap_win, page_rows, key_width),
        "blk",
        split_axis=0,
        concat_axis=0,
        tiled=True,
    )
    cached = received[arrival]
    new_owner = append_table // per_owner
    new_rank = earlier_same(new_owner)
    mine_owner = lax.dynamic_index_in_dim(new_owner, my_block, 0, keepdims=False)
    mine_rank = lax.dynamic_index_in_dim(new_rank, my_block, 0, keepdims=False)
    dest_wanted = (mine_owner[None, None, :] == jnp.arange(blocks)[:, None, None]) & (
        mine_rank[None, None, :] == jnp.arange(cap_new)[None, :, None]
    )
    page_pick = jnp.sum(jnp.where(dest_wanted, jnp.arange(new_pages)[None, None, :], 0), axis=2)
    page_live = jnp.any(dest_wanted, axis=2)
    fresh_pages = fresh_keys.reshape(new_pages, page_rows, key_width)
    parcels = jnp.where(page_live[:, :, None, None], fresh_pages[page_pick], 0)
    arrived = lax.all_to_all(
        parcels.reshape(blocks * cap_new, page_rows, key_width),
        "blk",
        split_axis=0,
        concat_axis=0,
        tiled=True,
    )
    land_wanted = (new_owner == my_block)[:, None, :] & (
        new_rank[:, None, :] == jnp.arange(cap_new)[None, :, None]
    )
    land_ids = pick_rows(land_wanted, append_table % per_owner)
    land_live = jnp.any(land_wanted, axis=2)
    targets = jnp.where(land_live, land_ids, per_owner).reshape(-1)
    new_pool = kv_pool.at[targets].set(arrived, mode="drop")
    keys_all = jnp.concatenate([cached.reshape(win_rows, key_width), fresh_keys], axis=0)
    own_length = lax.dynamic_index_in_dim(cache_lengths, my_block, 0, keepdims=False)
    filled = jnp.minimum(own_length // page_rows, win_pages)
    key_index = jnp.arange(win_rows + append_rows)
    live_keys = (key_index >= win_rows) | (key_index // page_rows >= win_pages - filled)
    block_len = min(128, tok_rows)
    block_count = tok_rows // block_len
    query_blocks = queries[0].reshape(block_count, block_len, queries.shape[2])
    first_row = piece_index * tok_rows
    offsets = jnp.arange(block_count) * block_len

    def one_block(inputs):
        qblock, offset = inputs
        block_start = first_row + offset
        return attend(
            qblock, keys_all, key_index, live_keys, block_start, head_count, head_size, win_rows
        )

    attended = lax.map(one_block, (query_blocks, offsets))
    attn_out = attended.reshape(1, tok_rows, queries.shape[2])
    return (attn_out, new_pool)


def solution(mesh):
    in_specs = (
        P("blk", "group", None),
        P("blk", "group", None),
        P("blk", None, None),
        P(),
        P(),
        P(),
    )
    out_specs = (P("blk", "group", None), P("blk", None, None))
    return jax.shard_map(shards, mesh=mesh, in_specs=in_specs, out_specs=out_specs, check_vma=False)
```

profile of v0, /device:TPU:13, one launch (start us, length us, event | category | flops | bytes accessed | tf_op | source)
XLA Modules:
  0.0 249.2 jit_solution(13082711198995688565)
XLA Ops:
  7.2 0.0 copy-start.1
  7.2 0.0 copy-start.2
  7.2 4.7 %copy.51 = bf16[32,128,512]{2,1,0:T(8,128)(2,1)} copy(bf16[32,128,512]{2,1,0:T(8,128)(2,1)} %param.10) | data formatting | bytes 8388608
  11.8 0.0 copy-done.1
  11.8 0.0 copy-done.2
  11.9 0.1 convert_reduce_fusion
  12.1 4.9 %gather_fusion = bf16[32,128,512]{2,1,0:T(8,128)(2,1)} fusion(bf16[32,128,512]{2,1,0:T(8,128)(2,1)} %copy.51, s32[1024]{0:T(1024)S(1)} %pad_clamp_fusion.2), kind=kCustom, calls=%fused_computation | custom fusion | bytes 8388736 | tf_op jit(solution)/shard_map/gather | solution.py:68
  17.0 4.5 %broadcast_select_fusion.1 = bf16[32,128,512]{2,1,0:T(8,128)(2,1)} fusion(bf16[32,128,512]{2,1,0:T(8,128)(2,1)} %gather_fusion, pred[32]{0:T(512)(128)(4,1)S(1)} %get-tuple-element.118), kind=kLoop, calls=%fused_computation.41 | loop fusion | flops 2097152 | bytes 8388640 | tf_op jit(solution)/shard_map/jit(_where)/select_n | solution.py:68
  21.5 0.0 copy-start.4
  21.5 11.3 %all-to-all-start = ((bf16[32,128,512]{2,1,0:T(8,128)(2,1)}), bf16[32,128,512]{2,1,0:T(8,128)(2,1)}, u32[]{:S(2)}, u32[]{:S(2)}) async-start(bf16[32,128,512]{2,1,0:T(8,128)(2,1)} %broadcast_select_fusion.1), calls=%async_computation | async-start | bytes 8388608 | tf_op jit(solution)/shard_map/all_to_all | solution.py:69
  32.8 0.0 all-gather.2.cloned.1.call-start
  32.9 0.7 all-gather.2.cloned.1.call-update
  33.5 0.0 copy-done.4
  33.6 0.7 dynamic_slice.27
  36.8 0.2 dynamic-slice_reduce_fusion
  37.0 0.2 fusion.36
  37.2 0.2 add_reduce_fusion
  37.4 0.1 select_reduce_fusion
  37.5 0.1 fusion.35
  37.6 0.5 fusion.41
  38.1 26.2 %all-gather.2.cloned.1.call-done = bf16[1,2048,512]{2,1,0:T(8,128)(2,1)} async-done(((bf16[1,256,512]{2,1,0:T(8,128)(2,1)}), bf16[1,2048,512]{2,1,0:T(8,128)(2,1)}) %all-gather.2.cloned.1.call-update) | async-done | bytes 2097168 | tf_op jit(solution)/shard_map/all_gather | solution.py:56
  64.3 4.4 %gather_fusion.2 = bf16[32,128,512]{2,1,0:T(8,128)(2,1)} fusion(bf16[16,128,512]{2,1,0:T(8,128)(2,1)} %bitcast.50, s32[1024]{0:T(1024)S(1)} %pad_clamp_fusion), kind=kCustom, calls=%fused_computation.2 | custom fusion | bytes 8388736 | tf_op jit(solution)/shard_map/gather | solution.py:87
  68.7 4.5 %broadcast_select_fusion = bf16[32,128,512]{2,1,0:T(8,128)(2,1)} fusion(bf16[32,128,512]{2,1,0:T(8,128)(2,1)} %gather_fusion.2, pred[32]{0:T(512)(128)(4,1)S(1)} %fusion.35), kind=kLoop, calls=%fused_computation.40 | loop fusion | flops 2097152 | bytes 8388640 | tf_op jit(solution)/shard_map/jit(_where)/select_n | solution.py:87
  73.2 54.1 %all-to-all-done = bf16[32,128,512]{2,1,0:T(8,128)(2,1)} async-done(((bf16[32,128,512]{2,1,0:T(8,128)(2,1)}), bf16[32,128,512]{2,1,0:T(8,128)(2,1)}, u32[]{:S(2)}, u32[]{:S(2)}) %all-to-all-start) | async-done | bytes 4194336 | tf_op jit(solution)/shard_map/all_to_all | solution.py:69
  127.4 6.9 %all-to-all-start.1 = ((bf16[32,128,512]{2,1,0:T(8,128)(2,1)}), bf16[32,128,512]{2,1,0:T(8,128)(2,1)}, u32[]{:S(2)}, u32[]{:S(2)}) async-start(bf16[32,128,512]{2,1,0:T(8,128)(2,1)} %broadcast_select_fusion), calls=%async_computation.1 | async-start | bytes 8388608 | tf_op jit(solution)/shard_map/all_to_all | solution.py:88
  134.3 0.0 copy-start
  134.3 4.3 %gather_fusion.1 = bf16[16,128,512]{2,1,0:T(8,128)(2,1)} fusion(bf16[32,128,512]{2,1,0:T(8,128)(2,1)} %all-to-all-done, s32[1024]{0:T(1024)S(1)} %pad_clamp_fusion.1), kind=kCustom, calls=%fused_computation.1 | custom fusion | bytes 4194368 | tf_op jit(solution)/shard_map/gather | solution.py:76
  138.6 0.0 copy-done
  138.6 3.8 %pad_maximum_fusion = bf16[4096,512]{1,0:T(8,128)(2,1)} fusion(bf16[2048,512]{1,0:T(8,128)(2,1)S(1)} %bitcast.51, bf16[2048,512]{1,0:T(8,128)(2,1)} %bitcast.53), kind=kLoop, calls=%fused_computation.39 | loop fusion | flops 8388608 | bytes 8388608 | tf_op jit(solution)/shard_map/concatenate | solution.py:102
  142.5 0.0 copy-start.3
  142.5 45.2 %while.12 = (s32[]{:T(128)}, bf16[2,128,2560]{2,1,0:T(8,128)(2,1)}, s32[2]{0:T(128)S(1)}, s32[]{:T(128)}, bf16[2,128,2560]{2,1,0:T(8,128)(2,1)}, /*index=5*/bf16[4096,512]{1,0:T(8,128)(2,1)}, s32[]{:T(128)}, s32[]{:T(128)}) while((s32[]{:T(128)}, bf16[2,128,2560]{2,1,0:T(8,128)(2,1)}, s32[2]{0:T(128)S(1)}, s32[]{:T(128)}, ...), condition=%wide.region_6.7_spmd.clone.clone, body=%wide.region_3.6_spmd.clone.clone.sunk | while | flops 5429176320 | bytes 77106312 | solution.py:120
  142.5 0.6 dynamic_slice.47
  143.7 0.6 fusion.56
  144.3 1.1 constant_dynamic-slice_fusion.2
  145.4 0.3 copy.38
  145.8 5.1 %fusion.57 = (f32[128,10]{0,1:T(8,128)S(1)}, f32[128,10,4096]{2,0,1:T(8,128)S(1)}) fusion(pred[128,4096]{1,0:T(8,128)(4,1)S(1)} %fusion.56, bf16[128,10,256]{0,2,1:T(8,128)(2,1)S(1)} %bitcast.52, bf16[4096,512]{1,0:T(8,128)(2,1)} %get-tuple-element.198), kind=kOutput, calls=%fused_computation.8.clone.1 | convolution fusion | flops 2700081920 | bytes 24253440 | tf_op jit(solution)/shard_map/while/body/eval_jaxpr/thd,kd->thk/dot_general | solution.py:21
  150.9 6.0 %fusion.58 = f32[128,10]{0,1:T(8,128)S(1)} fusion(f32[128,10,4096]{2,0,1:T(8,128)S(1)} %get-tuple-element.175, f32[128,10]{0,1:T(8,128)S(1)} %get-tuple-element.176, pred[128,4096]{1,0:T(8,128)(4,1)S(1)} %fusion.56), kind=kLoop, calls=%fused_computation.9.clone.1 | loop fusion | flops 20970240 | bytes 21506048 | tf_op jit(solution)/shard_map/while/body/eval_jaxpr/reduce_sum | solution.py:33
  156.9 6.7 %divide_convert_fusion.2 = bf16[128,10,256]{2,0,1:T(8,128)(2,1)S(1)} fusion(bf16[4096,512]{1,0:T(8,128)(2,1)} %get-tuple-element.198, f32[128,10,4096]{2,0,1:T(8,128)S(1)} %get-tuple-element.175, f32[128,10]{0,1:T(8,128)S(1)} %get-tuple-element.176, pred[128,4096]{1,0:T(8,128)(4,1)S(1)} %fusion.56, f32[128,10]{0,1:T(8,128)S(1)} %fusion.58), kind=kOutput, calls=%fused_computation.22.clone.1 | convolution fusion | flops 2705981440 | bytes 24258560 | tf_op jit(solution)/shard_map/while/body/eval_jaxpr/thk,kd->thd/dot_general | solution.py:35
  163.6 0.3 copy.39
  163.9 0.2 copy.40
  164.2 0.9 constant_dynamic-update-slice_fusion.2
  165.1 0.6 dynamic_slice.47
  166.3 0.6 fusion.56
  166.9 1.1 constant_dynamic-slice_fusion.2
  168.0 0.3 copy.38
  168.4 5.1 %fusion.57 = (f32[128,10]{0,1:T(8,128)S(1)}, f32[128,10,4096]{2,0,1:T(8,128)S(1)}) fusion(pred[128,4096]{1,0:T(8,128)(4,1)S(1)} %fusion.56, bf16[128,10,256]{0,2,1:T(8,128)(2,1)S(1)} %bitcast.52, bf16[4096,512]{1,0:T(8,128)(2,1)} %get-tuple-element.198), kind=kOutput, calls=%fused_computation.8.clone.1 | convolution fusion | flops 2700081920 | bytes 24253440 | tf_op jit(solution)/shard_map/while/body/eval_jaxpr/thd,kd->thk/dot_general | solution.py:21
  173.4 6.0 %fusion.58 = f32[128,10]{0,1:T(8,128)S(1)} fusion(f32[128,10,4096]{2,0,1:T(8,128)S(1)} %get-tuple-element.175, f32[128,10]{0,1:T(8,128)S(1)} %get-tuple-element.176, pred[128,4096]{1,0:T(8,128)(4,1)S(1)} %fusion.56), kind=kLoop, calls=%fused_computation.9.clone.1 | loop fusion | flops 20970240 | bytes 21506048 | tf_op jit(solution)/shard_map/while/body/eval_jaxpr/reduce_sum | solution.py:33
  179.5 6.7 %divide_convert_fusion.2 = bf16[128,10,256]{2,0,1:T(8,128)(2,1)S(1)} fusion(bf16[4096,512]{1,0:T(8,128)(2,1)} %get-tuple-element.198, f32[128,10,4096]{2,0,1:T(8,128)S(1)} %get-tuple-element.175, f32[128,10]{0,1:T(8,128)S(1)} %get-tuple-element.176, pred[128,4096]{1,0:T(8,128)(4,1)S(1)} %fusion.56, f32[128,10]{0,1:T(8,128)S(1)} %fusion.58), kind=kOutput, calls=%fused_computation.22.clone.1 | convolution fusion | flops 2705981440 | bytes 24258560 | tf_op jit(solution)/shard_map/while/body/eval_jaxpr/thk,kd->thd/dot_general | solution.py:35
  186.2 0.3 copy.39
  186.5 0.2 copy.40
  186.8 0.9 constant_dynamic-update-slice_fusion.2
  187.7 44.0 %all-to-all-done.1 = bf16[32,128,512]{2,1,0:T(8,128)(2,1)} async-done(((bf16[32,128,512]{2,1,0:T(8,128)(2,1)}), bf16[32,128,512]{2,1,0:T(8,128)(2,1)}, u32[]{:S(2)}, u32[]{:S(2)}) %all-to-all-start.1) | async-done | bytes 4194336 | tf_op jit(solution)/shard_map/all_to_all | solution.py:88
  231.7 0.0 copy-done.3
  231.7 10.7 %scatter_fusion = bf16[32,128,512]{2,1,0:T(8,128)(2,1)} fusion(bf16[32,128,512]{2,1,0:T(8,128)(2,1)} %copy.51, s32[32]{0:T(128)S(1)} %copy-done.3, bf16[32,128,512]{2,1,0:T(8,128)(2,1)} %all-to-all-done.1), kind=kCustom, calls=%fused_computation.3 | custom fusion | bytes 12583040 | tf_op jit(solution)/shard_map/scatter | solution.py:101
  (18 shorter events, 0.2 us)
Async XLA Ops:
  7.2 4.7 %copy-start.1 = (s32[32,16]{0,1:T(8,128)S(1)}, s32[32,16]{0,1:T(8,128)}, u32[]{:S(2)}) copy-start(s32[32,16]{0,1:T(8,128)} %param.11) | copy-start | bytes 6148
  7.2 4.7 %copy-start.2 = (s32[32,16]{0,1:T(8,128)S(1)}, s32[32,16]{0,1:T(8,128)}, u32[]{:S(2)}) copy-start(s32[32,16]{0,1:T(8,128)} %param.12) | copy-start | bytes 6148
  21.5 12.1 %copy-start.4 = (s32[32]{0:T(128)S(1)}, s32[32]{0:T(128)}, u32[]{:S(2)}) copy-start(s32[32]{0:T(128)} %param.13) | copy-start | bytes 388
  21.5 105.9 %all-to-all-start = ((bf16[32,128,512]{2,1,0:T(8,128)(2,1)}), bf16[32,128,512]{2,1,0:T(8,128)(2,1)}, u32[]{:S(2)}, u32[]{:S(2)}) async-start(bf16[32,128,512]{2,1,0:T(8,128)(2,1)} %broadcast_select_fusion.1), calls=%async_computation | async-start | bytes 8388608 | tf_op jit(solution)/shard_map/all_to_all | solution.py:69
  32.8 31.5 %all-gather.2.cloned.1.call-start = ((), (), s32[]{:S(2)}) async-start(), calls=%async_computation.2 | async-start | bytes 2359296 | tf_op jit(solution)/shard_map/all_gather | solution.py:56
  127.4 104.3 %all-to-all-start.1 = ((bf16[32,128,512]{2,1,0:T(8,128)(2,1)}), bf16[32,128,512]{2,1,0:T(8,128)(2,1)}, u32[]{:S(2)}, u32[]{:S(2)}) async-start(bf16[32,128,512]{2,1,0:T(8,128)(2,1)} %broadcast_select_fusion), calls=%async_computation.1 | async-start | bytes 8388608 | tf_op jit(solution)/shard_map/all_to_all | solution.py:88
  134.3 4.4 %copy-start = (bf16[1,2048,512]{2,1,0:T(8,128)(2,1)S(1)}, bf16[1,2048,512]{2,1,0:T(8,128)(2,1)}, u32[]{:S(2)}) copy-start(bf16[1,2048,512]{2,1,0:T(8,128)(2,1)} %all-gather.2.cloned.1.call-done) | copy-start | bytes 6291460
  142.5 89.2 %copy-start.3 = (s32[32]{0:T(128)S(1)}, s32[32]{0:T(128)}, u32[]{:S(2)}) copy-start(s32[32]{0:T(128)} %fusion.41) | copy-start | bytes 388
Sparse Core Ops, SparseCore 0:
  35.5 28.8 all-gather.1
where the time goes:
time: 250 us; the launch traced here: 249 us
  waiting for transfers between devices  125 us (50%)
  local copies, waits for them, and re-layouts  36.9 us (15%)
  other arithmetic  27.3 us (11%)
  matrix products  23.6 us (9%)
  starting transfers between devices  18.3 us (7%)
  between operations  16.7 us (7%)
    all_to_all x1, waiting for transfers between devices, shards(): lax.all_to_all(outgoing.reshape(blocks * cap_win, page_rows, key_width),...  54.1 us
    all_to_all x1, waiting for transfers between devices, shards(): lax.all_to_all(parcels.reshape(blocks * cap_new, page_rows, key_width), '...  44 us
    all_gather x1, waiting for transfers between devices, shards(): fresh_keys = lax.all_gather(new_kv, 'group', axis=1, tiled=True)[0]  26.2 us
    dot_general x2, matrix products, attend(): jnp.einsum('thk,kd->thd', weights, keys_use[:, head_size:], preferred_ele...  13.4 us
    reduce_sum x2, other arithmetic, attend(): row_total = jnp.sum(raw_weights, axis=2, keepdims=True)  12 us
    all_to_all x1, starting transfers between devices, shards(): lax.all_to_all(outgoing.reshape(blocks * cap_win, page_rows, key_width),...  11.3 us
    scatter x1, local copies, waits for them, and re-layouts, shards(): new_pool = kv_pool.at[targets].set(arrived, mode='drop')  10.7 us
    dot_general x2, matrix products, attend(): jnp.einsum('thd,kd->thk', query_rows, keys_use[:, :head_size], preferred_...  10.2 us
  transfers between devices with their start and end apart: 3, of which 3 were waited for; matrix products, arithmetic and copies ran while one was open for 25% of the time, Pallas kernels for 0%

commit v1 on v0

--- a/solution.py
+++ b/solution.py
@@ -2,6 +2,19 @@
 import jax.numpy as jnp
 from jax import lax
 from jax.sharding import PartitionSpec as P
+
+
+def collect(x, axis, dim):
+    ways = lax.axis_size(axis)
+    up = [(d, (d + 1) % ways) for d in range(ways)]
+    down = [(d, (d - 1) % ways) for d in range(ways)]
+    earlier, later = ([x], [x])
+    for _ in range(ways // 2):
+        earlier.append(lax.ppermute(earlier[-1], axis, up))
+    for _ in range((ways - 1) // 2):
+        later.append(lax.ppermute(later[-1], axis, down))
+    line = jnp.concatenate([*earlier[::-1], *later[1:]], axis=dim)
+    return jnp.roll(line, (lax.axis_index(axis) - ways // 2) * x.shape[dim], axis=dim)
 
 
 def earlier_same(owners):
@@ -53,7 +66,7 @@
     win_rows = win_pages * page_rows
     cap_win = (win_pages + blocks - 1) // blocks
     cap_new = (new_pages + blocks - 1) // blocks
-    fresh_keys = lax.all_gather(new_kv, "group", axis=1, tiled=True)[0]
+    fresh_keys = collect(new_kv, "group", 1)[0]
     append_rows = fresh_keys.shape[0]
     win_owner = window_table // per_owner
     win_rank = earlier_same(win_owner)

time: 250 us -> 237 us (0.948)
  between operations: 16.7 us -> 3.18 us
  waiting for transfers between devices: 125 us -> 115 us
  starting transfers between devices: 18.3 us -> 27.7 us
  local copies, waits for them, and re-layouts: 36.9 us -> 40.3 us
    all_gather x1 -> x0, waiting for transfers between devices: 26.2 us -> none  [shards(): fresh_keys = lax.all_gather(new_kv, 'group', axis=1, tiled=True)[0]]
    ppermute x0 -> x7, waiting for transfers between devices: none -> 15.1 us  [the longest x4 9.13 us: collect(): earlier.append(lax.ppermute(earlier[-1], axis, up))]
    ppermute x0 -> x7, starting transfers between devices: none -> 9.51 us  [the longest x4 9.49 us: collect(): earlier.append(lax.ppermute(earlier[-1], axis, up))]
    unnamed x11 -> x30, local copies, waits for them, and re-layouts: 4.67 us -> 7.81 us
  transfers between devices with their start and end apart: 3 -> 9, of which waited for: 3 -> 6; matrix products, arithmetic and copies ran while one was open for 25% -> 26% of each run, Pallas kernels for 0% -> 0%
where the time goes in v1:
time: 237 us; the launch traced here: 236 us
  waiting for transfers between devices  115 us (49%)
  local copies, waits for them, and re-layouts  40.3 us (17%)
  starting transfers between devices  27.7 us (12%)
  other arithmetic  25.2 us (11%)
  matrix products  23.6 us (10%)
  between operations  3.18 us (1%)
    all_to_all x1, waiting for transfers between devices, shards(): lax.all_to_all(outgoing.reshape(blocks * cap_win, page_rows, key_width),...  55.3 us
    all_to_all x1, waiting for transfers between devices, shards(): lax.all_to_all(parcels.reshape(blocks * cap_new, page_rows, key_width), '...  44.1 us
    dot_general x2, matrix products, attend(): jnp.einsum('thk,kd->thd', weights, keys_use[:, head_size:], preferred_ele...  13.4 us
    reduce_sum x2, other arithmetic, attend(): row_total = jnp.sum(raw_weights, axis=2, keepdims=True)  12 us
    all_to_all x1, starting transfers between devices, shards(): lax.all_to_all(outgoing.reshape(blocks * cap_win, page_rows, key_width),...  11.3 us
    scatter x1, local copies, waits for them, and re-layouts, shards(): new_pool = kv_pool.at[targets].set(arrived, mode='drop')  10.7 us
    dot_general x2, matrix products, attend(): jnp.einsum('thd,kd->thk', query_rows, keys_use[:, :head_size], preferred_...  10.2 us
    ppermute x4, starting transfers between devices, collect(): earlier.append(lax.ppermute(earlier[-1], axis, up))  9.49 us
  transfers between devices with their start and end apart: 9, of which 6 were waited for; matrix products, arithmetic and copies ran while one was open for 26% of the time, Pallas kernels for 0%

profile of v1, /device:TPU:13, one launch (start us, length us, event | category | flops | bytes accessed | tf_op | source)
XLA Modules:
  0.0 235.9 jit_solution(7794596802201944410)
XLA Ops:
  0.6 0.0 copy-start.3
  0.6 0.0 copy-start.4
  0.7 4.7 %copy.66 = bf16[32,128,512]{2,1,0:T(8,128)(2,1)} copy(bf16[32,128,512]{2,1,0:T(8,128)(2,1)} %param.10) | data formatting | bytes 8388608
  5.3 0.0 copy-done.3
  5.3 0.0 copy-done.4
  5.3 0.1 convert_reduce_fusion
  5.6 5.0 %gather_fusion = bf16[32,128,512]{2,1,0:T(8,128)(2,1)} fusion(bf16[32,128,512]{2,1,0:T(8,128)(2,1)} %copy.66, s32[1024]{0:T(1024)S(1)} %pad_clamp_fusion.2), kind=kCustom, calls=%fused_computation | custom fusion | bytes 8388736 | tf_op jit(solution)/shard_map/gather | solution.py:81
  10.5 4.5 %broadcast_select_fusion.1 = bf16[32,128,512]{2,1,0:T(8,128)(2,1)} fusion(bf16[32,128,512]{2,1,0:T(8,128)(2,1)} %gather_fusion, pred[32]{0:T(512)(128)(4,1)S(1)} %get-tuple-element.118), kind=kLoop, calls=%fused_computation.41 | loop fusion | flops 2097152 | bytes 8388640 | tf_op jit(solution)/shard_map/jit(_where)/select_n | solution.py:81
  15.0 11.3 %all-to-all-start = ((bf16[32,128,512]{2,1,0:T(8,128)(2,1)}), bf16[32,128,512]{2,1,0:T(8,128)(2,1)}, u32[]{:S(2)}, u32[]{:S(2)}) async-start(bf16[32,128,512]{2,1,0:T(8,128)(2,1)} %broadcast_select_fusion.1), calls=%async_computation | async-start | bytes 8388608 | tf_op jit(solution)/shard_map/all_to_all | solution.py:82
  26.4 2.0 collective-permute-start
  28.4 0.0 collective-permute-start.4
  28.4 0.2 dynamic-slice_reduce_fusion
  28.6 0.2 fusion.36
  28.8 0.1 select_reduce_fusion
  28.9 0.1 fusion.35
  29.0 2.8 %collective-permute-done = bf16[1,256,512]{2,1,0:T(8,128)(2,1)S(1)} collective-permute-done((bf16[1,256,512]{2,1,0:T(8,128)(2,1)S(1)}, bf16[1,256,512]{2,1,0:T(8,128)(2,1)S(1)}, u32[]{:S(2)}, u32[]{:S(2)}) %collective-permute-start) | collective-permute-done | bytes 262176 | tf_op jit(solution)/shard_map/ppermute | solution.py:13
  31.7 2.5 %collective-permute-start.1 = (bf16[1,256,512]{2,1,0:T(8,128)(2,1)S(1)}, bf16[1,256,512]{2,1,0:T(8,128)(2,1)S(1)}, u32[]{:S(2)}, u32[]{:S(2)}) collective-permute-start(bf16[1,256,512]{2,1,0:T(8,128)(2,1)S(1)} %collective-permute-done), channel_id=1, source_target_pairs={{0,1},{1,2},{2,3},{3,4},{4,5},{5,6},{6,7},{7,0},{8,9},{9,10},{10,1... | collective-permute-start | bytes 786440 | tf_op jit(solution)/shard_map/ppermute | solution.py:13
  34.2 0.2 add_reduce_fusion
  34.4 3.1 %collective-permute-done.1 = bf16[1,256,512]{2,1,0:T(8,128)(2,1)S(1)} collective-permute-done((bf16[1,256,512]{2,1,0:T(8,128)(2,1)S(1)}, bf16[1,256,512]{2,1,0:T(8,128)(2,1)S(1)}, u32[]{:S(2)}, u32[]{:S(2)}) %collective-permute-start.1) | collective-permute-done | bytes 262176 | tf_op jit(solution)/shard_map/ppermute | solution.py:13
  37.5 2.5 %collective-permute-start.2 = (bf16[1,256,512]{2,1,0:T(8,128)(2,1)S(1)}, bf16[1,256,512]{2,1,0:T(8,128)(2,1)S(1)}, u32[]{:S(2)}, u32[]{:S(2)}) collective-permute-start(bf16[1,256,512]{2,1,0:T(8,128)(2,1)S(1)} %collective-permute-done.1), channel_id=1, source_target_pairs={{0,1},{1,2},{2,3},{3,4},{4,5},{5,6},{6,7},{7,0},{8,9},{9,10},{10,1... | collective-permute-start | bytes 786440 | tf_op jit(solution)/shard_map/ppermute | solution.py:13
  40.0 0.0 collective-permute-done.4
  40.0 0.0 collective-permute-start.5
  40.1 3.3 %collective-permute-done.2 = bf16[1,256,512]{2,1,0:T(8,128)(2,1)S(1)} collective-permute-done((bf16[1,256,512]{2,1,0:T(8,128)(2,1)S(1)}, bf16[1,256,512]{2,1,0:T(8,128)(2,1)S(1)}, u32[]{:S(2)}, u32[]{:S(2)}) %collective-permute-start.2) | collective-permute-done | bytes 262176 | tf_op jit(solution)/shard_map/ppermute | solution.py:13
  43.3 2.5 %collective-permute-start.3 = (bf16[1,256,512]{2,1,0:T(8,128)(2,1)S(1)}, bf16[1,256,512]{2,1,0:T(8,128)(2,1)S(1)}, u32[]{:S(2)}, u32[]{:S(2)}) collective-permute-start(bf16[1,256,512]{2,1,0:T(8,128)(2,1)S(1)} %collective-permute-done.2), channel_id=1, source_target_pairs={{0,1},{1,2},{2,3},{3,4},{4,5},{5,6},{6,7},{7,0},{8,9},{9,10},{10,1... | collective-permute-start | bytes 786440 | tf_op jit(solution)/shard_map/ppermute | solution.py:13
  45.8 0.6 dynamic_slice.31
  48.7 0.5 fusion.41
  49.2 0.0 collective-permute-done.5
  49.2 0.0 collective-permute-start.6
  49.2 0.0 collective-permute-done.3
  49.4 6.0 %collective-permute-done.6 = bf16[1,256,512]{2,1,0:T(8,128)(2,1)S(1)} collective-permute-done((bf16[1,256,512]{2,1,0:T(8,128)(2,1)S(1)}, bf16[1,256,512]{2,1,0:T(8,128)(2,1)S(1)}, u32[]{:S(2)}, u32[]{:S(2)}) %collective-permute-start.6) | collective-permute-done | bytes 262176 | tf_op jit(solution)/shard_map/ppermute | solution.py:15
  55.7 0.0 copy-start.1
  55.7 1.9 copy-done.1
  57.6 0.1 constant_dynamic-slice_fusion.1
  57.7 2.8 %gather_fusion.2 = bf16[32,128,512]{2,1,0:T(8,128)(2,1)} fusion(bf16[16,128,512]{2,1,0:T(8,128)(2,1)S(1)} %bitcast.51, s32[1024]{0:T(1024)S(1)} %pad_clamp_fusion), kind=kCustom, calls=%fused_computation.2 | custom fusion | bytes 8388736 | tf_op jit(solution)/shard_map/gather | solution.py:100
  60.5 1.9 fusion.45
  62.4 0.9 copy-done
  63.3 2.3 broadcast_select_fusion
  65.6 55.3 %all-to-all-done = bf16[32,128,512]{2,1,0:T(8,128)(2,1)} async-done(((bf16[32,128,512]{2,1,0:T(8,128)(2,1)}), bf16[32,128,512]{2,1,0:T(8,128)(2,1)}, u32[]{:S(2)}, u32[]{:S(2)}) %all-to-all-start) | async-done | bytes 4194336 | tf_op jit(solution)/shard_map/all_to_all | solution.py:82
  120.9 6.9 %all-to-all-start.1 = ((bf16[32,128,512]{2,1,0:T(8,128)(2,1)}), bf16[32,128,512]{2,1,0:T(8,128)(2,1)}, u32[]{:S(2)}, u32[]{:S(2)}) async-start(bf16[32,128,512]{2,1,0:T(8,128)(2,1)} %broadcast_select_fusion), calls=%async_computation.1 | async-start | bytes 8388608 | tf_op jit(solution)/shard_map/all_to_all | solution.py:101
  127.8 4.2 %gather_fusion.1 = bf16[16,128,512]{2,1,0:T(8,128)(2,1)} fusion(bf16[32,128,512]{2,1,0:T(8,128)(2,1)} %all-to-all-done, s32[1024]{0:T(1024)S(1)} %pad_clamp_fusion.1), kind=kCustom, calls=%fused_computation.1 | custom fusion | bytes 4194368 | tf_op jit(solution)/shard_map/gather | solution.py:89
  132.0 3.8 %pad_maximum_fusion = bf16[4096,512]{1,0:T(8,128)(2,1)} fusion(bf16[2048,512]{1,0:T(8,128)(2,1)S(1)} %fusion.45, bf16[2048,512]{1,0:T(8,128)(2,1)} %bitcast.53), kind=kLoop, calls=%fused_computation.39 | loop fusion | flops 8388608 | bytes 8388608 | tf_op jit(solution)/shard_map/concatenate | solution.py:115
  135.9 45.2 %while.12 = (s32[]{:T(128)}, bf16[2,128,2560]{2,1,0:T(8,128)(2,1)}, s32[2]{0:T(128)S(1)}, s32[]{:T(128)}, bf16[2,128,2560]{2,1,0:T(8,128)(2,1)}, /*index=5*/bf16[4096,512]{1,0:T(8,128)(2,1)}, s32[]{:T(128)}, s32[]{:T(128)}) while((s32[]{:T(128)}, bf16[2,128,2560]{2,1,0:T(8,128)(2,1)}, s32[2]{0:T(128)S(1)}, s32[]{:T(128)}, ...), condition=%wide.region_6.7_spmd.clone.clone, body=%wide.region_3.6_spmd.clone.clone.sunk | while | flops 5429176320 | bytes 77106312 | solution.py:133
  135.9 0.6 dynamic_slice.55
  137.1 0.6 fusion.57
  137.7 1.1 constant_dynamic-slice_fusion.3
  138.8 0.3 copy.38
  139.2 5.1 %fusion.58 = (f32[128,10]{0,1:T(8,128)S(1)}, f32[128,10,4096]{2,0,1:T(8,128)S(1)}) fusion(pred[128,4096]{1,0:T(8,128)(4,1)S(1)} %fusion.57, bf16[128,10,256]{0,2,1:T(8,128)(2,1)S(1)} %bitcast.52, bf16[4096,512]{1,0:T(8,128)(2,1)} %get-tuple-element.198), kind=kOutput, calls=%fused_computation.8.clone.1 | convolution fusion | flops 2700081920 | bytes 24253440 | tf_op jit(solution)/shard_map/while/body/eval_jaxpr/thd,kd->thk/dot_general | solution.py:34
  144.3 6.0 %fusion.59 = f32[128,10]{0,1:T(8,128)S(1)} fusion(f32[128,10,4096]{2,0,1:T(8,128)S(1)} %get-tuple-element.175, f32[128,10]{0,1:T(8,128)S(1)} %get-tuple-element.176, pred[128,4096]{1,0:T(8,128)(4,1)S(1)} %fusion.57), kind=kLoop, calls=%fused_computation.9.clone.1 | loop fusion | flops 20970240 | bytes 21506048 | tf_op jit(solution)/shard_map/while/body/eval_jaxpr/reduce_sum | solution.py:46
  150.3 6.7 %divide_convert_fusion.2 = bf16[128,10,256]{2,0,1:T(8,128)(2,1)S(1)} fusion(bf16[4096,512]{1,0:T(8,128)(2,1)} %get-tuple-element.198, f32[128,10,4096]{2,0,1:T(8,128)S(1)} %get-tuple-element.175, f32[128,10]{0,1:T(8,128)S(1)} %get-tuple-element.176, pred[128,4096]{1,0:T(8,128)(4,1)S(1)} %fusion.57, f32[128,10]{0,1:T(8,128)S(1)} %fusion.59), kind=kOutput, calls=%fused_computation.22.clone.1 | convolution fusion | flops 2705981440 | bytes 24258560 | tf_op jit(solution)/shard_map/while/body/eval_jaxpr/thk,kd->thd/dot_general | solution.py:48
  157.0 0.3 copy.39
  157.3 0.2 copy.40
  157.6 0.9 constant_dynamic-update-slice_fusion.18
  158.5 0.6 dynamic_slice.55
  159.7 0.6 fusion.57
  160.3 1.1 constant_dynamic-slice_fusion.3
  161.4 0.3 copy.38
  161.8 5.1 %fusion.58 = (f32[128,10]{0,1:T(8,128)S(1)}, f32[128,10,4096]{2,0,1:T(8,128)S(1)}) fusion(pred[128,4096]{1,0:T(8,128)(4,1)S(1)} %fusion.57, bf16[128,10,256]{0,2,1:T(8,128)(2,1)S(1)} %bitcast.52, bf16[4096,512]{1,0:T(8,128)(2,1)} %get-tuple-element.198), kind=kOutput, calls=%fused_computation.8.clone.1 | convolution fusion | flops 2700081920 | bytes 24253440 | tf_op jit(solution)/shard_map/while/body/eval_jaxpr/thd,kd->thk/dot_general | solution.py:34
  166.9 6.0 %fusion.59 = f32[128,10]{0,1:T(8,128)S(1)} fusion(f32[128,10,4096]{2,0,1:T(8,128)S(1)} %get-tuple-element.175, f32[128,10]{0,1:T(8,128)S(1)} %get-tuple-element.176, pred[128,4096]{1,0:T(8,128)(4,1)S(1)} %fusion.57), kind=kLoop, calls=%fused_computation.9.clone.1 | loop fusion | flops 20970240 | bytes 21506048 | tf_op jit(solution)/shard_map/while/body/eval_jaxpr/reduce_sum | solution.py:46
  172.9 6.7 %divide_convert_fusion.2 = bf16[128,10,256]{2,0,1:T(8,128)(2,1)S(1)} fusion(bf16[4096,512]{1,0:T(8,128)(2,1)} %get-tuple-element.198, f32[128,10,4096]{2,0,1:T(8,128)S(1)} %get-tuple-element.175, f32[128,10]{0,1:T(8,128)S(1)} %get-tuple-element.176, pred[128,4096]{1,0:T(8,128)(4,1)S(1)} %fusion.57, f32[128,10]{0,1:T(8,128)S(1)} %fusion.59), kind=kOutput, calls=%fused_computation.22.clone.1 | convolution fusion | flops 2705981440 | bytes 24258560 | tf_op jit(solution)/shard_map/while/body/eval_jaxpr/thk,kd->thd/dot_general | solution.py:48
  179.6 0.3 copy.39
  179.9 0.2 copy.40
  180.2 0.9 constant_dynamic-update-slice_fusion.18
  181.1 44.1 %all-to-all-done.1 = bf16[32,128,512]{2,1,0:T(8,128)(2,1)} async-done(((bf16[32,128,512]{2,1,0:T(8,128)(2,1)}), bf16[32,128,512]{2,1,0:T(8,128)(2,1)}, u32[]{:S(2)}, u32[]{:S(2)}) %all-to-all-start.1) | async-done | bytes 4194336 | tf_op jit(solution)/shard_map/all_to_all | solution.py:101
  225.2 10.7 %scatter_fusion = bf16[32,128,512]{2,1,0:T(8,128)(2,1)} fusion(bf16[32,128,512]{2,1,0:T(8,128)(2,1)} %copy.66, s32[32]{0:T(128)S(1)} %copy-done.5, bf16[32,128,512]{2,1,0:T(8,128)(2,1)} %all-to-all-done.1), kind=kCustom, calls=%fused_computation.3 | custom fusion | bytes 12583040 | tf_op jit(solution)/shard_map/scatter | solution.py:114
  (41 shorter events, 0.5 us)
Async XLA Ops:
  0.6 4.7 %copy-start.3 = (s32[32,16]{0,1:T(8,128)S(1)}, s32[32,16]{0,1:T(8,128)}, u32[]{:S(2)}) copy-start(s32[32,16]{0,1:T(8,128)} %param.11) | copy-start | bytes 6148
  0.6 4.7 %copy-start.4 = (s32[32,16]{0,1:T(8,128)S(1)}, s32[32,16]{0,1:T(8,128)}, u32[]{:S(2)}) copy-start(s32[32,16]{0,1:T(8,128)} %param.12) | copy-start | bytes 6148
  15.0 11.3 %copy-start.2 = (bf16[1,256,512]{2,1,0:T(8,128)(2,1)S(1)}, bf16[1,256,512]{2,1,0:T(8,128)(2,1)}, u32[]{:S(2)}) copy-start(bf16[1,256,512]{2,1,0:T(8,128)(2,1)} %param.9) | copy-start | bytes 786436
  15.0 30.8 %copy-start.6 = (s32[32]{0:T(128)S(1)}, s32[32]{0:T(128)}, u32[]{:S(2)}) copy-start(s32[32]{0:T(128)} %param.13) | copy-start | bytes 388
  15.0 105.9 %all-to-all-start = ((bf16[32,128,512]{2,1,0:T(8,128)(2,1)}), bf16[32,128,512]{2,1,0:T(8,128)(2,1)}, u32[]{:S(2)}, u32[]{:S(2)}) async-start(bf16[32,128,512]{2,1,0:T(8,128)(2,1)} %broadcast_select_fusion.1), calls=%async_computation | async-start | bytes 8388608 | tf_op jit(solution)/shard_map/all_to_all | solution.py:82
  26.4 5.4 %collective-permute-start = (bf16[1,256,512]{2,1,0:T(8,128)(2,1)S(1)}, bf16[1,256,512]{2,1,0:T(8,128)(2,1)S(1)}, u32[]{:S(2)}, u32[]{:S(2)}) collective-permute-start(bf16[1,256,512]{2,1,0:T(8,128)(2,1)S(1)} %copy-done.2), channel_id=1, source_target_pairs={{0,1},{1,2},{2,3},{3,4},{4,5},{5,6},{6,7},{7,0},{8,9},{9,10},{10,1... | collective-permute-start | bytes 786440 | tf_op jit(solution)/shard_map/ppermute | solution.py:13
  28.4 11.6 %collective-permute-start.4 = (bf16[1,256,512]{2,1,0:T(8,128)(2,1)S(1)}, bf16[1,256,512]{2,1,0:T(8,128)(2,1)S(1)}, u32[]{:S(2)}, u32[]{:S(2)}) collective-permute-start(bf16[1,256,512]{2,1,0:T(8,128)(2,1)S(1)} %copy-done.2), channel_id=1, source_target_pairs={{0,7},{1,0},{2,1},{3,2},{4,3},{5,4},{6,5},{7,6},{8,15},{9,8},{10,9... | collective-permute-start | bytes 786440 | tf_op jit(solution)/shard_map/ppermute | solution.py:15
  31.7 5.8 %collective-permute-start.1 = (bf16[1,256,512]{2,1,0:T(8,128)(2,1)S(1)}, bf16[1,256,512]{2,1,0:T(8,128)(2,1)S(1)}, u32[]{:S(2)}, u32[]{:S(2)}) collective-permute-start(bf16[1,256,512]{2,1,0:T(8,128)(2,1)S(1)} %collective-permute-done), channel_id=1, source_target_pairs={{0,1},{1,2},{2,3},{3,4},{4,5},{5,6},{6,7},{7,0},{8,9},{9,10},{10,1... | collective-permute-start | bytes 786440 | tf_op jit(solution)/shard_map/ppermute | solution.py:13
  37.5 5.8 %collective-permute-start.2 = (bf16[1,256,512]{2,1,0:T(8,128)(2,1)S(1)}, bf16[1,256,512]{2,1,0:T(8,128)(2,1)S(1)}, u32[]{:S(2)}, u32[]{:S(2)}) collective-permute-start(bf16[1,256,512]{2,1,0:T(8,128)(2,1)S(1)} %collective-permute-done.1), channel_id=1, source_target_pairs={{0,1},{1,2},{2,3},{3,4},{4,5},{5,6},{6,7},{7,0},{8,9},{9,10},{10,1... | collective-permute-start | bytes 786440 | tf_op jit(solution)/shard_map/ppermute | solution.py:13
  40.0 9.2 %collective-permute-start.5 = (bf16[1,256,512]{2,1,0:T(8,128)(2,1)S(1)}, bf16[1,256,512]{2,1,0:T(8,128)(2,1)S(1)}, u32[]{:S(2)}, u32[]{:S(2)}) collective-permute-start(bf16[1,256,512]{2,1,0:T(8,128)(2,1)S(1)} %collective-permute-done.4), channel_id=1, source_target_pairs={{0,7},{1,0},{2,1},{3,2},{4,3},{5,4},{6,5},{7,6},{8,15},{9,8},{10,9... | collective-permute-start | bytes 786440 | tf_op jit(solution)/shard_map/ppermute | solution.py:15
  43.3 5.9 %collective-permute-start.3 = (bf16[1,256,512]{2,1,0:T(8,128)(2,1)S(1)}, bf16[1,256,512]{2,1,0:T(8,128)(2,1)S(1)}, u32[]{:S(2)}, u32[]{:S(2)}) collective-permute-start(bf16[1,256,512]{2,1,0:T(8,128)(2,1)S(1)} %collective-permute-done.2), channel_id=1, source_target_pairs={{0,1},{1,2},{2,3},{3,4},{4,5},{5,6},{6,7},{7,0},{8,9},{9,10},{10,1... | collective-permute-start | bytes 786440 | tf_op jit(solution)/shard_map/ppermute | solution.py:13
  49.2 6.2 %collective-permute-start.6 = (bf16[1,256,512]{2,1,0:T(8,128)(2,1)S(1)}, bf16[1,256,512]{2,1,0:T(8,128)(2,1)S(1)}, u32[]{:S(2)}, u32[]{:S(2)}) collective-permute-start(bf16[1,256,512]{2,1,0:T(8,128)(2,1)S(1)} %collective-permute-done.5), channel_id=1, source_target_pairs={{0,7},{1,0},{2,1},{3,2},{4,3},{5,4},{6,5},{7,6},{8,15},{9,8},{10,9... | collective-permute-start | bytes 786440 | tf_op jit(solution)/shard_map/ppermute | solution.py:15
  55.7 1.9 copy-start.1
  60.5 2.8 %copy-start = (bf16[32,128,512]{2,1,0:T(8,128)(2,1)S(1)}, bf16[32,128,512]{2,1,0:T(8,128)(2,1)}, u32[]{:S(2)}) copy-start(bf16[32,128,512]{2,1,0:T(8,128)(2,1)} %gather_fusion.2) | copy-start | bytes 12582916
  120.9 104.3 %all-to-all-start.1 = ((bf16[32,128,512]{2,1,0:T(8,128)(2,1)}), bf16[32,128,512]{2,1,0:T(8,128)(2,1)}, u32[]{:S(2)}, u32[]{:S(2)}) async-start(bf16[32,128,512]{2,1,0:T(8,128)(2,1)} %broadcast_select_fusion), calls=%async_computation.1 | async-start | bytes 8388608 | tf_op jit(solution)/shard_map/all_to_all | solution.py:101
  135.9 89.3 %copy-start.5 = (s32[32]{0:T(128)S(1)}, s32[32]{0:T(128)}, u32[]{:S(2)}) copy-start(s32[32]{0:T(128)} %fusion.41) | copy-start | bytes 388
